TPU v7x, 32 devices: a whole 2x2x4 slice. The times are simulated.
32 devices in a mesh: grp: 2 (over x), blade: 8 (over z, y), dof: 2 (over core).
Axes of the slice: x: 2, y: 2, z: 4, core: 2. Of those that a mesh axis runs over, the one named last changes fastest.
Arguments:
- panel: bfloat16 [8192, 512], P(('grp', 'blade', 'dof')), parts along dimension 0, may hold values from -0.25 to 0.25
- stiffness: bfloat16 [96, 64, 128, 128], P(('grp', 'blade'), 'dof'), parts along dimension 0, may hold values from -0.5 to 0.5
- block_rows: int32 [96, 64], P(('grp', 'blade'), 'dof'), parts along dimension 0, may hold values from 0 to 31
- block_cols: int32 [96, 64], P(('grp', 'blade'), 'dof'), parts along dimension 0, may hold values from 0 to 31
Outputs:
- spectral: float32 [2, 96, 512, 512], P(None, ('grp', 'blade'), 'dof'), parts along dimension 1
There are 2 independent parts, one for each index of `grp`. A program takes and returns all parts, laid end to end along the dimension named above; each array names one. Nothing has to cross between parts.
Inputs may be any that keep to these rules, and one draw needn't show every extreme that they name: `block_rows`: row block index of each stiffness block; indices of one blade may repeat. `block_cols`: column block index of each stiffness block; indices of one blade may repeat.
All inputs are finite; a program needn't handle non-finite values.
Results may differ from a plain program's by a relative error of at most 0.0029.
Values may be sent and summed in bfloat16 or wider, within the bound.
No kernel may reach another device: no remote copies, remote signals or barrier semaphores. Data moves between devices by JAX's collectives and lax.ppermute only.
A program may use at most 128 MiB of HBM per device.

v0:
```python
import math
import jax
import jax.numpy as jnp
from jax import lax
from jax.sharding import PartitionSpec as P


def body(panel, stiffness, block_rows, block_cols):
    block_size = stiffness.shape[-1]
    modes = panel.shape[-1]
    whole = lax.all_gather(panel, ("blade", "dof"), axis=0, tiled=True)
    blocks = whole.reshape(-1, block_size, modes)

    def one_blade(items):
        mats, rows, cols = items
        chosen = jnp.take(blocks, cols, axis=0)
        image = jnp.einsum("nij,njm->nim", mats, chosen, preferred_element_type=jnp.float32)
        image = image.astype(jnp.bfloat16)
        left = jnp.take(blocks, rows, axis=0).reshape(-1, modes)
        return lax.dot_general(
            left,
            image.reshape(-1, modes),
            (((0,), (0,)), ((), ())),
            preferred_element_type=jnp.float32,
        )

    partial_proj = lax.map(one_blade, (stiffness, block_rows, block_cols))
    blade_count = stiffness.shape[0] * lax.axis_size("blade")
    index = jnp.arange(blade_count, dtype=jnp.int32)
    angle = (index[:, None] * index[None, :] % blade_count).astype(jnp.float32) * (
        2.0 * math.pi / blade_count
    )
    cosine = jnp.cos(angle)
    sine = jnp.sin(angle)
    stacked = lax.all_to_all(partial_proj, "blade", split_axis=1, concat_axis=0, tiled=True)
    real_part = jnp.einsum("hb,brc->hrc", cosine, stacked, precision=lax.Precision.HIGHEST)
    imag_part = -jnp.einsum("hb,brc->hrc", sine, stacked, precision=lax.Precision.HIGHEST)
    joined = jnp.stack([real_part, imag_part])
    full_spec = lax.all_to_all(joined, "blade", split_axis=1, concat_axis=2, tiled=True)
    result = lax.psum_scatter(full_spec, "dof", scatter_dimension=2, tiled=True)
    return result


def solution(mesh):
    placed = (
        P(("grp", "blade", "dof"), None),
        P(("grp", "blade"), "dof", None, None),
        P(("grp", "blade"), "dof"),
        P(("grp", "blade"), "dof"),
    )
    return jax.shard_map(
        body,
        mesh=mesh,
        in_specs=placed,
        out_specs=P(None, ("grp", "blade"), "dof", None),
        check_vma=False,
    )
```

profile of v0, /device:TPU:0, one launch (start us, length us, event | category | flops | bytes accessed | tf_op | source)
XLA Modules:
  0.0 863.4 jit_solution(7075036304253567163)
XLA Ops:
  6.5 0.0 all-gather.2.cloned.1.call-start
  6.5 0.7 all-gather.2.cloned.1.call-update
  7.3 0.0 reduce-scatter.2.cloned.1.call-start
  7.3 55.5 %all-gather.2.cloned.1.call-done = bf16[4096,512]{1,0:T(8,128)(2,1)} async-done(((bf16[256,512]{1,0:T(8,128)(2,1)}), bf16[4096,512]{1,0:T(8,128)(2,1)}) %all-gather.2.cloned.1.call-update) | async-done | bytes 4194320 | tf_op jit(solution)/shard_map/all_gather | solution.py:11
  62.8 244.8 %while.10 = (s32[]{:T(128)}, f32[6,512,512]{2,0,1:T(8,128)}, s32[6,32]{1,0:T(8,128)}, bf16[32,128,512]{2,1,0:T(8,128)(2,1)}, bf16[6,32,128,128]{3,2,1,0:T(8,128)...) while((s32[]{:T(128)}, f32[6,512,512]{2,0,1:T(8,128)}, s32[6,32]{1,0:T(8,128)}, ...), condition=%wide.region_1.3_spmd, body=%wide.region_0.2_spmd.sunk | while | flops 2690648576 | bytes 31466728 | solution.py:27
  62.8 0.7 compare_and_fusion.3
  63.5 4.9 gather_fusion.1
  68.5 5.0 gather_fusion
  73.5 7.2 fusion.71
  80.8 1.1 copy.41
  81.8 21.8 %dynamic_update_slice.5 = f32[6,512,512]{2,0,1:T(8,128)} dynamic-update-slice(f32[6,512,512]{2,0,1:T(8,128)} %get-tuple-element.111, f32[1,512,512]{2,0,1:T(1,128)S(1)} %copy.41, s32[]{:T(128)S(6)} %copy.45, s32[]{:T(128)} %constant.36.clone.1..sunk, s32[]{:T(128)} %constant.36.clone.1..sunk) | dynamic-update-slice | bytes 2097156 | tf_op jit(solution)/shard_map/while/body/jit(dynamic_update_index_in_dim)/dynamic_update_slice | solution.py:27
  103.6 0.7 compare_and_fusion.3
  104.3 4.9 gather_fusion.1
  109.3 5.0 gather_fusion
  114.3 7.2 fusion.71
  121.6 1.1 copy.41
  122.6 21.8 %dynamic_update_slice.5 = f32[6,512,512]{2,0,1:T(8,128)} dynamic-update-slice(f32[6,512,512]{2,0,1:T(8,128)} %get-tuple-element.111, f32[1,512,512]{2,0,1:T(1,128)S(1)} %copy.41, s32[]{:T(128)S(6)} %copy.45, s32[]{:T(128)} %constant.36.clone.1..sunk, s32[]{:T(128)} %constant.36.clone.1..sunk) | dynamic-update-slice | bytes 2097156 | tf_op jit(solution)/shard_map/while/body/jit(dynamic_update_index_in_dim)/dynamic_update_slice | solution.py:27
  144.4 0.7 compare_and_fusion.3
  145.1 4.9 gather_fusion.1
  150.1 5.0 gather_fusion
  155.1 7.2 fusion.71
  162.3 1.1 copy.41
  163.4 21.8 %dynamic_update_slice.5 = f32[6,512,512]{2,0,1:T(8,128)} dynamic-update-slice(f32[6,512,512]{2,0,1:T(8,128)} %get-tuple-element.111, f32[1,512,512]{2,0,1:T(1,128)S(1)} %copy.41, s32[]{:T(128)S(6)} %copy.45, s32[]{:T(128)} %constant.36.clone.1..sunk, s32[]{:T(128)} %constant.36.clone.1..sunk) | dynamic-update-slice | bytes 2097156 | tf_op jit(solution)/shard_map/while/body/jit(dynamic_update_index_in_dim)/dynamic_update_slice | solution.py:27
  185.2 0.7 compare_and_fusion.3
  185.9 4.9 gather_fusion.1
  190.9 5.0 gather_fusion
  195.9 7.2 fusion.71
  203.1 1.1 copy.41
  204.2 21.8 %dynamic_update_slice.5 = f32[6,512,512]{2,0,1:T(8,128)} dynamic-update-slice(f32[6,512,512]{2,0,1:T(8,128)} %get-tuple-element.111, f32[1,512,512]{2,0,1:T(1,128)S(1)} %copy.41, s32[]{:T(128)S(6)} %copy.45, s32[]{:T(128)} %constant.36.clone.1..sunk, s32[]{:T(128)} %constant.36.clone.1..sunk) | dynamic-update-slice | bytes 2097156 | tf_op jit(solution)/shard_map/while/body/jit(dynamic_update_index_in_dim)/dynamic_update_slice | solution.py:27
  226.0 0.7 compare_and_fusion.3
  226.7 4.9 gather_fusion.1
  231.7 5.0 gather_fusion
  236.7 7.2 fusion.71
  243.9 1.1 copy.41
  245.0 21.8 %dynamic_update_slice.5 = f32[6,512,512]{2,0,1:T(8,128)} dynamic-update-slice(f32[6,512,512]{2,0,1:T(8,128)} %get-tuple-element.111, f32[1,512,512]{2,0,1:T(1,128)S(1)} %copy.41, s32[]{:T(128)S(6)} %copy.45, s32[]{:T(128)} %constant.36.clone.1..sunk, s32[]{:T(128)} %constant.36.clone.1..sunk) | dynamic-update-slice | bytes 2097156 | tf_op jit(solution)/shard_map/while/body/jit(dynamic_update_index_in_dim)/dynamic_update_slice | solution.py:27
  266.8 0.7 compare_and_fusion.3
  267.5 4.9 gather_fusion.1
  272.5 5.0 gather_fusion
  277.5 7.2 fusion.71
  284.7 1.1 copy.41
  285.8 21.8 %dynamic_update_slice.5 = f32[6,512,512]{2,0,1:T(8,128)} dynamic-update-slice(f32[6,512,512]{2,0,1:T(8,128)} %get-tuple-element.111, f32[1,512,512]{2,0,1:T(1,128)S(1)} %copy.41, s32[]{:T(128)S(6)} %copy.45, s32[]{:T(128)} %constant.36.clone.1..sunk, s32[]{:T(128)} %constant.36.clone.1..sunk) | dynamic-update-slice | bytes 2097156 | tf_op jit(solution)/shard_map/while/body/jit(dynamic_update_index_in_dim)/dynamic_update_slice | solution.py:27
  307.6 187.5 %all_to_all.36 = f32[6,512,512]{2,0,1:T(8,128)S(1)} all-to-all(f32[6,512,512]{2,0,1:T(8,128)} %get-tuple-element.38), channel_id=1, replica_groups=mesh['grp'=2,'blade'=8,'dof'=2] {'blade'}, dimensions={1} | all-to-all | bytes 12582912 | tf_op jit(solution)/shard_map/all_to_all | solution.py:35
  495.1 3.6 copy.21
  498.6 9.7 %negate_bitcast_fusion = f32[1,48,64,512]{3,1,2,0:T(8,128)S(1)} fusion(f32[48,64,512]{2,1,0:T(8,128)S(1)} %bitcast.41), kind=kOutput, calls=%fused_computation.26 | convolution fusion | flops 907563264 | bytes 12582912 | tf_op jit(solution)/shard_map/hb,brc->hrc/dot_general | solution.py:37
  508.3 10.2 %fusion.34 = f32[1,48,64,512]{3,1,2,0:T(8,128)} fusion(f32[48,64,512]{2,1,0:T(8,128)S(1)} %bitcast.42), kind=kOutput, calls=%fused_computation.31 | convolution fusion | flops 905990400 | bytes 12582912 | tf_op jit(solution)/shard_map/hb,brc->hrc/dot_general | solution.py:36
  518.5 9.5 %pad_maximum_fusion = f32[2,48,64,512]{3,1,2,0:T(8,128)} fusion(f32[1,48,64,512]{3,1,2,0:T(8,128)S(1)} %negate_bitcast_fusion, f32[1,48,64,512]{3,1,2,0:T(8,128)} %fusion.34), kind=kLoop, calls=%fused_computation.25 | loop fusion | flops 3145728 | bytes 25165824 | tf_op jit(solution)/shard_map/stack | solution.py:38
  528.0 16.4 %copy.24 = f32[2,48,64,512]{3,2,0,1:T(8,128)} copy(f32[2,48,64,512]{3,1,2,0:T(8,128)} %pad_maximum_fusion) | data formatting | bytes 25165824 | tf_op jit(solution)/shard_map/stack | solution.py:38
  544.4 279.6 %all_to_all.37 = f32[2,48,64,512]{3,2,0,1:T(8,128)} all-to-all(f32[2,48,64,512]{3,2,0,1:T(8,128)} %copy.24), channel_id=1, replica_groups=mesh['grp'=2,'blade'=8,'dof'=2] {'blade'}, dimensions={1} | all-to-all | bytes 25165824 | tf_op jit(solution)/shard_map/all_to_all | solution.py:39
  823.9 12.0 %copy.26 = f32[2,6,8,64,512]{4,3,2,1,0:T(8,128)} copy(f32[2,6,8,64,512]{4,3,0,1,2:T(8,128)} %bitcast.44) | data formatting | bytes 25165824 | tf_op jit(solution)/shard_map/all_to_all | solution.py:39
  835.9 0.0 reduce-scatter.2.cloned.1.call-update
  835.9 20.6 %reduce-scatter.2.cloned.1.call-done = f32[2,6,256,512]{3,2,1,0:T(8,128)} async-done(((f32[2,6,512,512]{3,2,1,0:T(8,128)}), f32[2,6,256,512]{3,2,1,0:T(8,128)}) %reduce-scatter.2.cloned.1.call-update) | async-done | bytes 6291472 | tf_op jit(solution)/shard_map/reduce_scatter | solution.py:40
  (13 shorter events, 0.1 us)
Async XLA Ops:
  6.5 56.3 %all-gather.2.cloned.1.call-start = ((), (), s32[]{:S(2)}) async-start(), calls=%async_computation.3 | async-start | bytes 4456448 | tf_op jit(solution)/shard_map/all_gather | solution.py:11
  7.3 849.3 %reduce-scatter.2.cloned.1.call-start = ((), (), s32[]{:S(2)}) async-start(), calls=%async_computation.4 | async-start | bytes 18874368 | tf_op jit(solution)/shard_map/reduce_scatter | solution.py:40
Sparse Core Ops, SparseCore 0:
  9.5 53.2 all-gather.1
  836.0 20.4 reduce-scatter.1
where the time goes:
time: 868 us; the launch traced here: 863 us
  blocking collectives  467 us (54%)
  local copies, waits for them, and re-layouts  229 us (26%)
  waiting for transfers between devices  76.9 us (9%)
  matrix products  63.3 us (7%)
  other arithmetic  13.8 us (2%)
  between operations  13.4 us (2%)
    all_to_all x1, blocking collectives, body(): lax.all_to_all(joined, 'blade', split_axis=1, concat_axis=2, tiled=True)  280 us
    all_to_all x1, blocking collectives, body(): lax.all_to_all(partial_proj, 'blade', split_axis=1, concat_axis=0, tiled=...  187 us
    dynamic_update_slice x12, local copies, waits for them, and re-layouts, body(): partial_proj = lax.map(one_blade, (stiffness, block_rows, block_cols))  137 us
    all_gather x1, waiting for transfers between devices, body(): whole = lax.all_gather(panel, ('blade', 'dof'), axis=0, tiled=True)  55.5 us
    dot_general x6, matrix products, one_blade(): lax.dot_general(left, image.reshape(-1, modes), (((0,), (0,)), ((), ())),...  43.5 us
    gather x6, local copies, waits for them, and re-layouts, one_blade(): chosen = jnp.take(blocks, cols, axis=0)  30.1 us
    gather x6, local copies, waits for them, and re-layouts, one_blade(): left = jnp.take(blocks, rows, axis=0).reshape(-1, modes)  29.7 us
    reduce_scatter x1, waiting for transfers between devices, body(): result = lax.psum_scatter(full_spec, 'dof', scatter_dimension=2, tiled=True)  20.6 us
  transfers between devices with their start and end apart: 2, of which 2 were waited for; matrix products, arithmetic and copies ran while one was open for 0% of the time, Pallas kernels for 0%

commit v1 on v0

--- a/solution.py
+++ b/solution.py
@@ -36,7 +36,9 @@
     real_part = jnp.einsum("hb,brc->hrc", cosine, stacked, precision=lax.Precision.HIGHEST)
     imag_part = -jnp.einsum("hb,brc->hrc", sine, stacked, precision=lax.Precision.HIGHEST)
     joined = jnp.stack([real_part, imag_part])
-    full_spec = lax.all_to_all(joined, "blade", split_axis=1, concat_axis=2, tiled=True)
+    shards = jnp.split(joined, lax.axis_size("blade"), axis=1)
+    received = lax.all_to_all(jnp.stack(shards), "blade", 0, 0)
+    full_spec = jnp.concatenate(received, axis=2)
     result = lax.psum_scatter(full_spec, "dof", scatter_dimension=2, tiled=True)
     return result
 

time: 868 us -> 879 us (1.013)
    unnamed x0 -> x7, other arithmetic: none -> 12.2 us
where the time goes in v1:
time: 879 us; the launch traced here: 871 us
  blocking collectives  467 us (53%)
  local copies, waits for them, and re-layouts  232 us (26%)
  waiting for transfers between devices  76.9 us (9%)
  matrix products  62.8 us (7%)
  other arithmetic  18.2 us (2%)
  between operations  13.7 us (2%)
    all_to_all x1, blocking collectives, body(): received = lax.all_to_all(jnp.stack(shards), 'blade', 0, 0)  280 us
    all_to_all x1, blocking collectives, body(): lax.all_to_all(partial_proj, 'blade', split_axis=1, concat_axis=0, tiled=...  187 us
    dynamic_update_slice x12, local copies, waits for them, and re-layouts, body(): partial_proj = lax.map(one_blade, (stiffness, block_rows, block_cols))  137 us
    all_gather x1, waiting for transfers between devices, body(): whole = lax.all_gather(panel, ('blade', 'dof'), axis=0, tiled=True)  55.5 us
    dot_general x6, matrix products, one_blade(): lax.dot_general(left, image.reshape(-1, modes), (((0,), (0,)), ((), ())),...  43.5 us
    gather x6, local copies, waits for them, and re-layouts, one_blade(): chosen = jnp.take(blocks, cols, axis=0)  30.1 us
    gather x6, local copies, waits for them, and re-layouts, one_blade(): left = jnp.take(blocks, rows, axis=0).reshape(-1, modes)  29.7 us
    reduce_scatter x1, waiting for transfers between devices, body(): result = lax.psum_scatter(full_spec, 'dof', scatter_dimension=2, tiled=True)  20.6 us
  transfers between devices with their start and end apart: 2, of which 2 were waited for; matrix products, arithmetic and copies ran while one was open for 0% of the time, Pallas kernels for 0%

profile of v1, /device:TPU:0, one launch (start us, length us, event | category | flops | bytes accessed | tf_op | source)
XLA Modules:
  0.0 871.0 jit_solution(15680265137471495586)
XLA Ops:
  6.5 0.0 all-gather.2.cloned.1.call-start
  6.5 0.7 all-gather.2.cloned.1.call-update
  7.3 0.0 reduce-scatter.2.cloned.1.call-start
  7.3 55.5 %all-gather.2.cloned.1.call-done = bf16[4096,512]{1,0:T(8,128)(2,1)} async-done(((bf16[256,512]{1,0:T(8,128)(2,1)}), bf16[4096,512]{1,0:T(8,128)(2,1)}) %all-gather.2.cloned.1.call-update) | async-done | bytes 4194320 | tf_op jit(solution)/shard_map/all_gather | solution.py:11
  62.8 244.8 %while.10 = (s32[]{:T(128)}, f32[6,512,512]{2,0,1:T(8,128)}, s32[6,32]{1,0:T(8,128)}, bf16[32,128,512]{2,1,0:T(8,128)(2,1)}, bf16[6,32,128,128]{3,2,1,0:T(8,128)...) while((s32[]{:T(128)}, f32[6,512,512]{2,0,1:T(8,128)}, s32[6,32]{1,0:T(8,128)}, ...), condition=%wide.region_1.3_spmd, body=%wide.region_0.2_spmd.sunk | while | flops 2690648576 | bytes 31466728 | solution.py:27
  62.8 0.7 compare_and_fusion.3
  63.6 4.9 gather_fusion.1
  68.5 5.0 gather_fusion
  73.5 7.2 fusion.94
  80.8 1.1 copy.37
  81.9 21.8 %dynamic_update_slice.5 = f32[6,512,512]{2,0,1:T(8,128)} dynamic-update-slice(f32[6,512,512]{2,0,1:T(8,128)} %get-tuple-element.111, f32[1,512,512]{2,0,1:T(1,128)S(1)} %copy.37, s32[]{:T(128)S(6)} %copy.41, s32[]{:T(128)} %constant.36.clone.1..sunk, s32[]{:T(128)} %constant.36.clone.1..sunk) | dynamic-update-slice | bytes 2097156 | tf_op jit(solution)/shard_map/while/body/jit(dynamic_update_index_in_dim)/dynamic_update_slice | solution.py:27
  103.6 0.7 compare_and_fusion.3
  104.4 4.9 gather_fusion.1
  109.3 5.0 gather_fusion
  114.3 7.2 fusion.94
  121.6 1.1 copy.37
  122.7 21.8 %dynamic_update_slice.5 = f32[6,512,512]{2,0,1:T(8,128)} dynamic-update-slice(f32[6,512,512]{2,0,1:T(8,128)} %get-tuple-element.111, f32[1,512,512]{2,0,1:T(1,128)S(1)} %copy.37, s32[]{:T(128)S(6)} %copy.41, s32[]{:T(128)} %constant.36.clone.1..sunk, s32[]{:T(128)} %constant.36.clone.1..sunk) | dynamic-update-slice | bytes 2097156 | tf_op jit(solution)/shard_map/while/body/jit(dynamic_update_index_in_dim)/dynamic_update_slice | solution.py:27
  144.4 0.7 compare_and_fusion.3
  145.2 4.9 gather_fusion.1
  150.1 5.0 gather_fusion
  155.1 7.2 fusion.94
  162.4 1.1 copy.37
  163.5 21.8 %dynamic_update_slice.5 = f32[6,512,512]{2,0,1:T(8,128)} dynamic-update-slice(f32[6,512,512]{2,0,1:T(8,128)} %get-tuple-element.111, f32[1,512,512]{2,0,1:T(1,128)S(1)} %copy.37, s32[]{:T(128)S(6)} %copy.41, s32[]{:T(128)} %constant.36.clone.1..sunk, s32[]{:T(128)} %constant.36.clone.1..sunk) | dynamic-update-slice | bytes 2097156 | tf_op jit(solution)/shard_map/while/body/jit(dynamic_update_index_in_dim)/dynamic_update_slice | solution.py:27
  185.2 0.7 compare_and_fusion.3
  186.0 4.9 gather_fusion.1
  190.9 5.0 gather_fusion
  195.9 7.2 fusion.94
  203.2 1.1 copy.37
  204.3 21.8 %dynamic_update_slice.5 = f32[6,512,512]{2,0,1:T(8,128)} dynamic-update-slice(f32[6,512,512]{2,0,1:T(8,128)} %get-tuple-element.111, f32[1,512,512]{2,0,1:T(1,128)S(1)} %copy.37, s32[]{:T(128)S(6)} %copy.41, s32[]{:T(128)} %constant.36.clone.1..sunk, s32[]{:T(128)} %constant.36.clone.1..sunk) | dynamic-update-slice | bytes 2097156 | tf_op jit(solution)/shard_map/while/body/jit(dynamic_update_index_in_dim)/dynamic_update_slice | solution.py:27
  226.0 0.7 compare_and_fusion.3
  226.8 4.9 gather_fusion.1
  231.7 5.0 gather_fusion
  236.7 7.2 fusion.94
  244.0 1.1 copy.37
  245.1 21.8 %dynamic_update_slice.5 = f32[6,512,512]{2,0,1:T(8,128)} dynamic-update-slice(f32[6,512,512]{2,0,1:T(8,128)} %get-tuple-element.111, f32[1,512,512]{2,0,1:T(1,128)S(1)} %copy.37, s32[]{:T(128)S(6)} %copy.41, s32[]{:T(128)} %constant.36.clone.1..sunk, s32[]{:T(128)} %constant.36.clone.1..sunk) | dynamic-update-slice | bytes 2097156 | tf_op jit(solution)/shard_map/while/body/jit(dynamic_update_index_in_dim)/dynamic_update_slice | solution.py:27
  266.8 0.7 compare_and_fusion.3
  267.6 4.9 gather_fusion.1
  272.5 5.0 gather_fusion
  277.5 7.2 fusion.94
  284.8 1.1 copy.37
  285.9 21.8 %dynamic_update_slice.5 = f32[6,512,512]{2,0,1:T(8,128)} dynamic-update-slice(f32[6,512,512]{2,0,1:T(8,128)} %get-tuple-element.111, f32[1,512,512]{2,0,1:T(1,128)S(1)} %copy.37, s32[]{:T(128)S(6)} %copy.41, s32[]{:T(128)} %constant.36.clone.1..sunk, s32[]{:T(128)} %constant.36.clone.1..sunk) | dynamic-update-slice | bytes 2097156 | tf_op jit(solution)/shard_map/while/body/jit(dynamic_update_index_in_dim)/dynamic_update_slice | solution.py:27
  307.6 187.5 %all_to_all.23 = f32[6,512,512]{2,0,1:T(8,128)S(1)} all-to-all(f32[6,512,512]{2,0,1:T(8,128)} %get-tuple-element.38), channel_id=1, replica_groups=mesh['grp'=2,'blade'=8,'dof'=2] {'blade'}, dimensions={1} | all-to-all | bytes 12582912 | tf_op jit(solution)/shard_map/all_to_all | solution.py:35
  495.1 3.6 copy.19
  498.7 9.7 %negate_bitcast_fusion = f32[1,48,64,512]{3,1,2,0:T(8,128)S(1)} fusion(f32[48,64,512]{2,1,0:T(8,128)S(1)} %bitcast.72), kind=kOutput, calls=%fused_computation.39 | convolution fusion | flops 907563264 | bytes 12582912 | tf_op jit(solution)/shard_map/hb,brc->hrc/dot_general | solution.py:37
  508.4 9.6 %fusion.34 = f32[1,48,64,512]{3,1,2,0:T(8,128)S(1)} fusion(f32[48,64,512]{2,1,0:T(8,128)S(1)} %bitcast.73), kind=kOutput, calls=%fused_computation.44 | convolution fusion | flops 905990400 | bytes 12582912 | tf_op jit(solution)/shard_map/hb,brc->hrc/dot_general | solution.py:36
  518.0 1.6 fusion.44
  519.5 1.8 fusion.47
  521.3 1.8 fusion.50
  523.1 1.6 fusion.53
  524.8 1.6 fusion.56
  526.3 1.8 fusion.59
  528.1 2.0 fusion.41
  530.2 1.6 fusion.61
  531.8 20.0 %copy.22 = f32[8,2,6,64,512]{4,3,2,1,0:T(8,128)} copy(f32[8,2,6,64,512]{4,2,3,1,0:T(8,128)} %fusion.61) | data formatting | bytes 25165824 | tf_op jit(solution)/shard_map/stack | solution.py:40
  551.8 279.6 %all_to_all.24 = f32[8,2,6,64,512]{4,3,2,1,0:T(8,128)} all-to-all(f32[8,2,6,64,512]{4,3,2,1,0:T(8,128)} %copy.22), channel_id=1, replica_groups=mesh['grp'=2,'blade'=8,'dof'=2] {'blade'}, dimensions={0} | all-to-all | bytes 25165824 | tf_op jit(solution)/shard_map/all_to_all | solution.py:40
  831.3 11.9 %copy.23 = f32[8,2,6,64,512]{4,3,0,2,1:T(8,128)} copy(f32[8,2,6,64,512]{4,3,2,1,0:T(8,128)} %all_to_all.24) | data formatting | bytes 25165824 | tf_op jit(solution)/shard_map/all_to_all | solution.py:40
  843.2 0.0 reduce-scatter.2.cloned.1.call-update
  843.3 20.6 %reduce-scatter.2.cloned.1.call-done = f32[2,6,256,512]{3,2,1,0:T(8,128)} async-done(((f32[2,6,512,512]{3,2,1,0:T(8,128)}), f32[2,6,256,512]{3,2,1,0:T(8,128)}) %reduce-scatter.2.cloned.1.call-update) | async-done | bytes 6291472 | tf_op jit(solution)/shard_map/reduce_scatter | solution.py:42
  (13 shorter events, 0.1 us)
Async XLA Ops:
  6.5 56.3 %all-gather.2.cloned.1.call-start = ((), (), s32[]{:S(2)}) async-start(), calls=%async_computation.3 | async-start | bytes 4456448 | tf_op jit(solution)/shard_map/all_gather | solution.py:11
  7.3 856.6 %reduce-scatter.2.cloned.1.call-start = ((), (), s32[]{:S(2)}) async-start(), calls=%async_computation.4 | async-start | bytes 18874368 | tf_op jit(solution)/shard_map/reduce_scatter | solution.py:42
Sparse Core Ops, SparseCore 0:
  9.5 53.2 all-gather.1
  843.4 20.4 reduce-scatter.1
